TPU v7x, 256 devices: a whole 4x4x8 slice. The times are simulated.
256 devices in a mesh: row: 32 (over z, y_hi, core), col: 8 (over y_lo, x).
Axes of the slice: x: 4, y: 4 (y_hi: 2, y_lo: 2; y = y_hi * 2 + y_lo), z: 8, core: 2. Of those that a mesh axis runs over, the one named last changes fastest.
Arguments:
- factor: float32 [49152, 8192], P('row', 'col'), may hold values from -0.0546875 to 0.0546875
- covariance: float32 [49152, 2048], P('row', 'col'), may hold values from -6 to 6
- inv_diagonal: float32 [8192], P(('col', 'row')), may hold values from 0.5 to 4
- columns: int32 [2048], replicated, may hold values from 0 to 8191
Outputs:
- sigma_window: float32 [8192, 2048], P(('col', 'row'))
Inputs may be any that keep to these rules, and one draw needn't show every extreme that they name: `columns`: each entry is a separator index; entries may repeat.
All inputs are finite; a program needn't handle non-finite values.
Results may differ from a plain program's by a relative error of at most 0.000071.
Values sent between devices are 32-bit elements; how exact they have to be, the bound alone decides.
No kernel may reach another device: no remote copies, remote signals or barrier semaphores. Data moves between devices by JAX's collectives and lax.ppermute only.
A program may use at most 128 MiB of HBM per device.

v0:
```python
import jax
import jax.numpy as jnp
from jax import lax
from jax.sharding import PartitionSpec as P


def contract_rows(left_block, right_block):
    return lax.dot_general(
        left_block,
        right_block,
        (((0,), (0,)), ((), ())),
        precision=lax.Precision.HIGHEST,
        preferred_element_type=jnp.float32,
    )


def per_device(factor, covariance, inv_diagonal, columns):
    row_devices = lax.axis_size("row")
    gathered = lax.all_gather(covariance, "col", axis=1, tiled=True)
    product = lax.psum_scatter(
        contract_rows(factor, gathered), "row", scatter_dimension=0, tiled=True
    )
    row_count = product.shape[0]
    block_index = lax.axis_index("col") * row_devices + lax.axis_index("row")
    row_ids = block_index * row_count + lax.iota(jnp.int32, row_count)
    on_diagonal = row_ids[:, None] == columns[None, :]
    return jnp.where(on_diagonal, inv_diagonal[:, None], jnp.zeros((), jnp.float32)) - product


def solution(mesh):
    return jax.shard_map(
        per_device,
        mesh=mesh,
        in_specs=(P("row", "col"), P("row", "col"), P(("col", "row")), P()),
        out_specs=P(("col", "row"), None),
        check_vma=False,
    )
```

profile of v0, /device:TPU:2, one launch (start us, length us, event | category | flops | bytes accessed | tf_op | source)
XLA Modules:
  0.0 352.7 jit_solution(8926620871789993303)
XLA Ops:
  6.5 0.0 all-gather.2.cloned.1.call-start
  6.5 0.7 all-gather.2.cloned.1.call-update
  7.3 0.0 reduce-scatter.2.cloned.1.call-start
  7.3 136.4 %all-gather.2.cloned.1.call-done = f32[1536,2048]{1,0:T(8,128)} async-done(((f32[1536,256]{1,0:T(8,128)}), f32[1536,2048]{1,0:T(8,128)}) %all-gather.2.cloned.1.call-update) | async-done | bytes 12582928 | tf_op jit(solution)/shard_map/all_gather | solution.py:19
  143.7 44.9 %fusion = f32[1024,2048]{1,0:T(8,128)} fusion(f32[1536,1024]{1,0:T(8,128)} %param.4, f32[1536,2048]{1,0:T(8,128)} %all-gather.2.cloned.1.call-done), kind=kOutput, calls=%fused_computation.2 | convolution fusion | flops 38654705664 | bytes 27262976 | tf_op jit(solution)/shard_map/dot_general | solution.py:8
  188.7 0.0 copy-start
  188.7 0.0 copy-start.1
  188.7 0.0 reduce-scatter.2.cloned.1.call-update
  188.7 155.3 %reduce-scatter.2.cloned.1.call-done = f32[32,2048]{1,0:T(8,128)} async-done(((f32[1024,2048]{1,0:T(8,128)}), f32[32,2048]{1,0:T(8,128)}) %reduce-scatter.2.cloned.1.call-update) | async-done | bytes 262160 | tf_op jit(solution)/shard_map/reduce_scatter | solution.py:20
  344.1 0.0 copy-done
  344.1 0.0 copy-done.1
  344.1 1.7 select_subtract_fusion
  (1 shorter events, 0.0 us)
Async XLA Ops:
  6.5 137.2 %all-gather.2.cloned.1.call-start = ((), (), s32[]{:S(2)}) async-start(), calls=%async_computation.1 | async-start | bytes 14155776 | tf_op jit(solution)/shard_map/all_gather | solution.py:19
  7.3 336.8 %reduce-scatter.2.cloned.1.call-start = ((), (), s32[]{:S(2)}) async-start(), calls=%async_computation.2 | async-start | bytes 8650752 | tf_op jit(solution)/shard_map/reduce_scatter | solution.py:20
  188.7 155.4 %copy-start = (s32[2048]{0:T(1024)S(1)}, s32[2048]{0:T(1024)}, u32[]{:S(2)}) copy-start(s32[2048]{0:T(1024)} %param.7) | copy-start | bytes 24580
  188.7 155.4 %copy-start.1 = (f32[32]{0:T(128)S(1)}, f32[32]{0:T(128)}, u32[]{:S(2)}) copy-start(f32[32]{0:T(128)} %param.6) | copy-start | bytes 388
Sparse Core Ops, SparseCore 0:
  9.1 134.5 all-gather.1
  188.8 155.1 reduce-scatter.1
where the time goes:
time: 353 us
  waiting for transfers between devices  292 us (83%)
  matrix products  44.9 us (13%)
  between operations  13.4 us (4%)
    reduce_scatter x1, waiting for transfers between devices, per_device(): lax.psum_scatter(contract_rows(factor, gathered), 'row', scatter_dimensio...  155 us
    all_gather x1, waiting for transfers between devices, per_device(): gathered = lax.all_gather(covariance, 'col', axis=1, tiled=True)  136 us
    dot_general x1, matrix products, contract_rows(): lax.dot_general(left_block, right_block, (((0,), (0,)), ((), ())), precis...  44.9 us
  transfers between devices with their start and end apart: 2, of which 2 were waited for; matrix products, arithmetic and copies ran while one was open for 0% of the time, Pallas kernels for 0%

commit v1 on v0

--- a/solution.py
+++ b/solution.py
@@ -16,7 +16,9 @@
 
 def per_device(factor, covariance, inv_diagonal, columns):
     row_devices = lax.axis_size("row")
-    gathered = lax.all_gather(covariance, "col", axis=1, tiled=True)
+    gathered = jnp.concatenate(
+        lax.all_to_all(jnp.stack([covariance] * lax.axis_size("col")), "col", 0, 0), axis=1
+    )
     product = lax.psum_scatter(
         contract_rows(factor, gathered), "row", scatter_dimension=0, tiled=True
     )

time: 353 us -> 402 us (1.14)
  blocking collectives: 0 us -> 146 us
  waiting for transfers between devices: 292 us -> 156 us
  matrix products: 44.9 us -> 82 us
    all_to_all x0 -> x1, blocking collectives: none -> 146 us  [per_device(): lax.all_to_all(jnp.stack([covariance] * lax.axis_size('col')), 'col', 0, 0)]
    all_gather x1 -> x0, waiting for transfers between devices: 136 us -> none  [per_device(): gathered = lax.all_gather(covariance, 'col', axis=1, tiled=True)]
    dot_general x1, matrix products: 44.9 us -> 82 us  [contract_rows(): lax.dot_general(left_block, right_block, (((0,), (0,)), ((), ())), precis...]
  transfers between devices with their start and end apart: 2 -> 1, of which waited for: 2 -> 1; matrix products, arithmetic and copies ran while one was open for 0% -> 0% of each run, Pallas kernels for 0% -> 0%
where the time goes in v1:
time: 402 us
  waiting for transfers between devices  156 us (39%)
  blocking collectives  146 us (36%)
  matrix products  82 us (20%)
  between operations  13.4 us (3%)
    reduce_scatter x1, waiting for transfers between devices, per_device(): lax.psum_scatter(contract_rows(factor, gathered), 'row', scatter_dimensio...  156 us
    all_to_all x1, blocking collectives, per_device(): lax.all_to_all(jnp.stack([covariance] * lax.axis_size('col')), 'col', 0, 0)  146 us
    dot_general x1, matrix products, contract_rows(): lax.dot_general(left_block, right_block, (((0,), (0,)), ((), ())), precis...  82 us
  transfers between devices with their start and end apart: 1, of which 1 were waited for; matrix products, arithmetic and copies ran while one was open for 0% of the time, Pallas kernels for 0%

profile of v1, /device:TPU:2, one launch (start us, length us, event | category | flops | bytes accessed | tf_op | source)
XLA Modules:
  0.0 402.1 jit_solution(17100753431786356676)
XLA Ops:
  6.5 0.0 reduce-scatter.2.cloned.1.call-start
  6.5 1.9 copy.5
  8.4 1.6 stack.2
  10.0 145.7 %all_to_all.5 = f32[8,1536,256]{1,2,0:T(8,128)S(1)} all-to-all(f32[8,1536,256]{1,2,0:T(8,128)S(1)} %stack.2), channel_id=1, replica_groups=mesh['row'=32,'col'=8] {'col'}, dimensions={0} | all-to-all | bytes 25165824 | tf_op jit(solution)/shard_map/all_to_all | solution.py:20
  155.8 82.0 %fusion = f32[1024,2048]{1,0:T(8,128)} fusion(f32[1536,1024]{1,0:T(8,128)} %param.4, f32[1536,2048]{0,1:T(8,128)S(1)} %bitcast.5), kind=kOutput, calls=%fused_computation.2 | convolution fusion | flops 38654705664 | bytes 27262976 | tf_op jit(solution)/shard_map/dot_general | solution.py:8
  237.7 0.0 copy-start
  237.7 0.0 copy-start.1
  237.7 0.0 reduce-scatter.2.cloned.1.call-update
  237.8 155.7 %reduce-scatter.2.cloned.1.call-done = f32[32,2048]{1,0:T(8,128)} async-done(((f32[1024,2048]{1,0:T(8,128)}), f32[32,2048]{1,0:T(8,128)}) %reduce-scatter.2.cloned.1.call-update) | async-done | bytes 262160 | tf_op jit(solution)/shard_map/reduce_scatter | solution.py:22
  393.5 0.0 copy-done
  393.5 0.0 copy-done.1
  393.5 1.7 select_subtract_fusion
  (1 shorter events, 0.0 us)
Async XLA Ops:
  6.5 386.9 %reduce-scatter.2.cloned.1.call-start = ((), (), s32[]{:S(2)}) async-start(), calls=%async_computation.2 | async-start | bytes 8650752 | tf_op jit(solution)/shard_map/reduce_scatter | solution.py:22
  237.7 155.7 %copy-start = (s32[2048]{0:T(1024)S(1)}, s32[2048]{0:T(1024)}, u32[]{:S(2)}) copy-start(s32[2048]{0:T(1024)} %param.7) | copy-start | bytes 24580
  237.7 155.7 %copy-start.1 = (f32[32]{0:T(128)S(1)}, f32[32]{0:T(128)}, u32[]{:S(2)}) copy-start(f32[32]{0:T(128)} %param.6) | copy-start | bytes 388
Sparse Core Ops, SparseCore 0:
  237.9 155.5 reduce-scatter.1
